TPU v7x, 256 devices: a whole 4x4x8 slice. The times are simulated.
256 devices in a mesh: req: 32 (over z, y_hi, core), tp: 8 (over x, y_lo).
Axes of the slice: x: 4, y: 4 (y_hi: 2, y_lo: 2; y = y_hi * 2 + y_lo), z: 8, core: 2. Of those that a mesh axis runs over, the one named last changes fastest.
Arguments:
- tokens: bfloat16 [16384, 1024], P(('req', 'tp')), may hold values from -6 to 6
- w_qkv: bfloat16 [1024, 3, 1024], P(None, None, 'tp'), may hold values from -0.1875 to 0.1875
- w_out: bfloat16 [1024, 1024], P('tp'), may hold values from -0.75 to 0.75
- w_up: bfloat16 [1024, 4096], P(None, 'tp'), may hold values from -0.1875 to 0.1875
- b_up: float32 [4096], P('tp'), may hold values from -4 to 4
- w_down: bfloat16 [4096, 1024], P('tp'), may hold values from -0.09375 to 0.09375
- b_down: float32 [1024], replicated, may hold values from -3 to 3
- ln1_gain: float32 [1024], replicated, may hold values from 0.5 to 1.5
- ln1_bias: float32 [1024], replicated, may hold values from -3 to 3
- ln2_gain: float32 [1024], replicated, may hold values from 0.5 to 1.5
- ln2_bias: float32 [1024], replicated, may hold values from -3 to 3
- kv_cache: bfloat16 [2, 32, 16384, 1024], P(None, None, 'req', 'tp'), may hold values from -122 to 122
- cache_len: int32 [32], replicated, may hold values from 0 to 16384, as said below
- span_len: int32 [32], replicated, may hold values from 1 to 512, as said below
Outputs:
- output: bfloat16 [16384, 1024], P(('req', 'tp'))
Inputs may be any that keep to these rules, and one draw needn't show every extreme that they name: The first cache_len[r] positions of request r hold its keys and values; some request has 16384. Slots from span_len[r] on are padding whose keys are not attended to; some request has 512.
All inputs are finite; a program needn't handle non-finite values.
Results may differ from a plain program's by a relative error of at most 0.015.
Values may be sent and summed in bfloat16 or wider, within the bound.
No kernel may reach another device: no remote copies, remote signals or barrier semaphores. Data moves between devices by JAX's collectives and lax.ppermute only.
A program may use at most 128 MiB of HBM per device.

v0:
```python
import jax
import jax.numpy as jnp
from jax import lax
from jax.sharding import PartitionSpec as P

HEAD_DIM = 64
BLOCK_GROUP = 4
masked_score = -1e30


def layer_norm(values, gain, bias):
    centre = jnp.mean(values, axis=-1, keepdims=True)
    centred = values - centre
    variance = jnp.mean(centred * centred, axis=-1, keepdims=True)
    return centred * lax.rsqrt(variance + 1e-05) * gain + bias


def partial_attention(queries, key_rows, value_rows, allowed):
    scores = jnp.einsum(
        "chd,nhd->hcn", queries, key_rows, preferred_element_type=jnp.float32
    ) * queries.shape[-1] ** (-0.5)
    scores = jnp.where(allowed[None], scores, masked_score)
    peaks = jnp.max(scores, axis=-1)
    weights = jnp.where(allowed[None], jnp.exp(scores - peaks[..., None]), 0.0).astype(jnp.bfloat16)
    weight_sums = jnp.sum(weights.astype(jnp.float32), axis=-1)
    blended = jnp.einsum("hcn,nhd->chd", weights, value_rows, preferred_element_type=jnp.float32)
    return (peaks.T, weight_sums.T, blended.reshape(blended.shape[0], -1))


def merge_axis(peaks, weight_sums, blended, axis):
    highest = jnp.max(peaks, axis=axis, keepdims=True)
    factors = jnp.exp(peaks - highest)
    sums_out = jnp.sum(factors * weight_sums, axis=axis)
    spread = jnp.repeat(factors, blended.shape[-1] // peaks.shape[-1], axis=-1)
    blend_out = jnp.sum(spread * blended, axis=axis)
    return (jnp.squeeze(highest, axis=axis), sums_out, blend_out)


def cache_partials(queries, keys, values, cached_count):
    total_blocks, block_width = (keys.shape[0], keys.shape[1])
    group = BLOCK_GROUP if total_blocks % BLOCK_GROUP == 0 else 1

    def single(one_keys, one_values, block):
        places = block * block_width + jnp.arange(block_width, dtype=jnp.int32)
        allowed = jnp.broadcast_to(
            (places < cached_count)[None, :], (queries.shape[0], block_width)
        )
        return partial_attention(queries, one_keys, one_values, allowed)

    def grouped(items):
        return jax.vmap(single)(*items)

    def regroup(member):
        return member.reshape((total_blocks // group, group) + member.shape[1:])

    results = lax.map(
        grouped,
        (regroup(keys), regroup(values), regroup(jnp.arange(total_blocks, dtype=jnp.int32))),
    )
    return tuple((member.reshape((total_blocks,) + member.shape[2:]) for member in results))


def shards(
    tokens,
    w_qkv,
    w_out,
    w_up,
    b_up,
    w_down,
    b_down,
    ln1_gain,
    ln1_bias,
    ln2_gain,
    ln2_bias,
    kv_cache,
    cache_len,
    span_len,
):
    width_here = w_qkv.shape[2]
    heads_here = width_here // HEAD_DIM
    where_req = lax.axis_index("req")
    own_cache = lax.all_to_all(kv_cache, "req", split_axis=1, concat_axis=1, tiled=True)
    span_rows = lax.all_gather(tokens, "tp", axis=0, tiled=True)
    flat_qkv = w_qkv.reshape(w_qkv.shape[0], 3 * width_here)
    heads_qkv = jnp.dot(span_rows, flat_qkv, preferred_element_type=jnp.float32).astype(
        jnp.bfloat16
    )
    span = heads_qkv.shape[0]
    local_shape = (span, heads_here, HEAD_DIM)
    queries = heads_qkv[:, :width_here].reshape(local_shape)
    fresh_keys = heads_qkv[:, width_here : 2 * width_here].reshape(local_shape)
    fresh_values = heads_qkv[:, 2 * width_here :].reshape(local_shape)
    full_out = lax.all_gather(w_out, "tp", axis=0, tiled=True)
    fresh_count = span_len[where_req]
    cached_count = cache_len[where_req]
    positions = jnp.arange(span, dtype=jnp.int32)
    allowed = (positions[None, :] <= positions[:, None]) & (positions[None, :] < fresh_count)
    fresh = partial_attention(queries, fresh_keys, fresh_values, allowed)
    total_blocks, block_width = (own_cache.shape[1], own_cache.shape[2])
    cached = own_cache.reshape(2, total_blocks, block_width, heads_here, HEAD_DIM)
    peaks, weight_sums, blended = cache_partials(queries, cached[0], cached[1], cached_count)
    peaks, weight_sums, blended = merge_axis(
        jnp.concatenate([fresh[0][None], peaks]),
        jnp.concatenate([fresh[1][None], weight_sums]),
        jnp.concatenate([fresh[2][None], blended]),
        0,
    )
    attention = (blended / jnp.repeat(weight_sums, HEAD_DIM, axis=-1)).astype(jnp.bfloat16)
    attention = lax.all_to_all(attention, "tp", split_axis=0, concat_axis=1, tiled=True)
    projected = jnp.dot(attention, full_out, preferred_element_type=jnp.float32)
    normed = layer_norm(tokens.astype(jnp.float32) + projected, ln1_gain, ln1_bias).astype(
        jnp.bfloat16
    )
    n_tp = lax.axis_size("tp")
    span_normed = lax.all_to_all(
        jnp.broadcast_to(normed[None], (n_tp,) + normed.shape),
        "tp",
        split_axis=0,
        concat_axis=0,
        tiled=True,
    ).reshape(-1, normed.shape[1])
    hidden = jax.nn.gelu(
        jnp.dot(span_normed, w_up, preferred_element_type=jnp.float32) + b_up, approximate=False
    ).astype(jnp.bfloat16)
    partial = jnp.dot(hidden, w_down, preferred_element_type=jnp.float32).astype(jnp.bfloat16)
    partial = lax.all_to_all(
        partial.reshape((n_tp, -1) + partial.shape[1:]),
        "tp",
        split_axis=0,
        concat_axis=0,
        tiled=True,
    )
    summed = jnp.sum(partial.astype(jnp.float32), axis=0) + b_down + normed.astype(jnp.float32)
    return layer_norm(summed, ln2_gain, ln2_bias).astype(jnp.bfloat16)


def solution(mesh):
    placed = (
        P(("req", "tp"), None),
        P(None, None, "tp"),
        P("tp", None),
        P(None, "tp"),
        P("tp"),
        P("tp", None),
        P(),
        P(),
        P(),
        P(),
        P(),
        P(None, None, "req", "tp"),
        P(),
        P(),
    )
    return jax.shard_map(
        shards, mesh=mesh, in_specs=placed, out_specs=P(("req", "tp"), None), check_vma=False
    )
```

profile of v0, /device:TPU:8, one launch (start us, length us, event | category | flops | bytes accessed | tf_op | source)
XLA Modules:
  0.0 363.8 jit_solution(2658030651955312103)
XLA Ops:
  6.5 12.1 %copy.29 = bf16[2,32,512,128]{2,3,0,1:T(8,128)(2,1)} copy(bf16[2,32,512,128]{3,2,1,0:T(8,128)(2,1)} %param.27) | data formatting | bytes 16777216 | tf_op args[11]
  18.6 10.9 %all-to-all-start = ((bf16[2,32,512,128]{2,3,0,1:T(8,128)(2,1)}), bf16[2,32,512,128]{2,3,0,1:T(8,128)(2,1)}, u32[]{:S(2)}, u32[]{:S(2)}) async-start(bf16[2,32,512,128]{2,3,0,1:T(8,128)(2,1)} %copy.29), calls=%async_computation | async-start | bytes 16777216 | tf_op jit(solution)/shard_map/all_to_all | solution.py:82
  33.3 64.3 %all-gather.3.cloned.1.call-done = bf16[512,1024]{1,0:T(8,128)(2,1)} async-done(((bf16[64,1024]{1,0:T(8,128)(2,1)}), bf16[512,1024]{1,0:T(8,128)(2,1)}) %all-gather.3.cloned.1.call-update) | async-done | bytes 1048592 | tf_op jit(solution)/shard_map/all_gather | solution.py:83
  101.5 111.0 %all-to-all-done = bf16[2,32,512,128]{2,3,0,1:T(8,128)(2,1)} async-done(((bf16[2,32,512,128]{2,3,0,1:T(8,128)(2,1)}), bf16[2,32,512,128]{2,3,0,1:T(8,128)(2,1)}, u32[]{:S(2)}, u32[]{:S(2)}) %all-to-all-start) | async-done | bytes 8388640 | tf_op jit(solution)/shard_map/all_to_all | solution.py:82
  212.5 5.9 %fusion.93 = (bf16[1,32,512,128]{2,3,0,1:T(8,128)(2,1)}, bf16[1,32,512,128]{2,3,0,1:T(8,128)(2,1)}) fusion(bf16[2,32,512,128]{2,3,0,1:T(8,128)(2,1)} %all-to-all-done), kind=kLoop, calls=%fused_computation.137 | loop fusion | bytes 16777216 | tf_op jit(solution)/shard_map/slice | solution.py:101
  218.4 74.6 %while.14 = (s32[]{:T(128)}, f32[8,4,512,2]{2,1,3,0:T(4,128)S(1)}, f32[8,4,512,2]{2,3,1,0:T(2,128)S(1)}, f32[8,4,512,128]{2,3,1,0:T(8,128)}, s32[8,4]{1,0:T(8,12...) while((s32[]{:T(128)}, f32[8,4,512,2]{2,1,3,0:T(4,128)S(1)}, ...), condition=%wide.region_4.5_spmd, body=%wide.region_1.4_spmd.sunk | while | flops 557838336 | bytes 29612216 | solution.py:56
  219.2 3.0 bitcast_reduce_fusion.2
  222.2 2.6 convert_reduce_fusion.4
  228.6 3.0 bitcast_reduce_fusion.2
  231.6 2.6 convert_reduce_fusion.4
  237.9 3.0 bitcast_reduce_fusion.2
  240.9 2.6 convert_reduce_fusion.4
  243.5 1.9 fusion.113
  247.2 3.0 bitcast_reduce_fusion.2
  250.2 2.6 convert_reduce_fusion.4
  252.8 1.9 fusion.113
  256.5 3.0 bitcast_reduce_fusion.2
  259.5 2.6 convert_reduce_fusion.4
  265.9 3.0 bitcast_reduce_fusion.2
  268.9 2.6 convert_reduce_fusion.4
  275.2 3.0 bitcast_reduce_fusion.2
  278.2 2.6 convert_reduce_fusion.4
  280.8 1.9 fusion.113
  284.5 3.0 bitcast_reduce_fusion.2
  287.5 2.6 convert_reduce_fusion.4
  293.3 4.1 %fusion.12 = f32[512,2,64]{0,2,1:T(8,128)S(1)} fusion(f32[32,512,2,64]{1,3,2,0:T(8,128)} %bitcast.103, f32[1,512,2,64]{1,3,2,0:T(8,128)S(1)} %convolution_bitcast_fusion, f32[33,512,2]{1,2,0:T(2,128)S(1)} %get-tuple-element.105), kind=kLoop, calls=%fused_computation.24 | loop fusion | flops 6422528 | bytes 9048064 | tf_op jit(solution)/shard_map/reduce_sum | solution.py:35
  298.5 10.8 %all-to-all-start.1 = ((bf16[8,64,128]{2,1,0:T(8,128)(2,1)}), bf16[8,64,128]{2,1,0:T(8,128)(2,1)S(1)}, u32[]{:S(2)}, u32[]{:S(2)}) async-start(bf16[8,64,128]{2,1,0:T(8,128)(2,1)} %copy.35), calls=%async_computation.1 | async-start | bytes 262144 | tf_op jit(solution)/shard_map/all_to_all | solution.py:109
  309.3 5.4 %all-to-all-done.1 = bf16[8,64,128]{2,1,0:T(8,128)(2,1)S(1)} async-done(((bf16[8,64,128]{2,1,0:T(8,128)(2,1)}), bf16[8,64,128]{2,1,0:T(8,128)(2,1)S(1)}, u32[]{:S(2)}, u32[]{:S(2)}) %all-to-all-start.1) | async-done | bytes 131104 | tf_op jit(solution)/shard_map/all_to_all | solution.py:109
  314.7 2.2 fusion.95
  317.4 17.2 %all_to_all.31 = bf16[8,64,1024]{2,1,0:T(8,128)(2,1)S(1)} all-to-all(bf16[8,64,1024]{2,1,0:T(8,128)(2,1)S(1)} %broadcast_in_dim.109), channel_id=1, replica_groups=mesh['req'=32,'tp'=8] {'tp'}, dimensions={0} | all-to-all | bytes 2097152 | tf_op jit(solution)/shard_map/all_to_all | solution.py:115
  334.6 4.6 %convolution_convert_fusion = bf16[512,1024]{1,0:T(8,128)(2,1)S(1)} fusion(bf16[512,1024]{1,0:T(8,128)(2,1)S(1)} %copy-done, bf16[512,1024]{1,0:T(8,128)(2,1)S(1)} %bitcast.107, bf16[1024,512]{1,0:T(8,128)(2,1)} %param.19, f32[512]{0:T(512)S(1)} %copy-done.8), kind=kOutput, calls=%fused_computation.31 | convolution fusion | flops 1091567616 | bytes 4196352 | tf_op jit(solution)/shard_map/dot_general | solution.py:125
  339.3 16.2 %all_to_all.32 = bf16[8,64,1024]{2,1,0:T(8,128)(2,1)S(1)} all-to-all(bf16[8,64,1024]{2,1,0:T(8,128)(2,1)S(1)} %bitcast.108), channel_id=1, replica_groups=mesh['req'=32,'tp'=8] {'tp'}, dimensions={0} | all-to-all | bytes 2097152 | tf_op jit(solution)/shard_map/all_to_all | solution.py:126
  (104 shorter events, 35.2 us)
Async XLA Ops:
  6.5 328.1 %copy-start = (bf16[512,1024]{1,0:T(8,128)(2,1)S(1)}, bf16[512,1024]{1,0:T(8,128)(2,1)}, u32[]{:S(2)}) copy-start(bf16[512,1024]{1,0:T(8,128)(2,1)} %param.21) | copy-start | bytes 3145732
  18.6 12.4 %copy-start.1 = (bf16[1024,3,128]{2,0,1:T(8,128)(2,1)S(1)}, bf16[1024,3,128]{2,0,1:T(8,128)(2,1)}, u32[]{:S(2)}) copy-start(bf16[1024,3,128]{2,0,1:T(8,128)(2,1)} %param.17) | copy-start | bytes 2359300
  18.6 12.7 %copy-start.9 = (s32[32]{0:T(128)S(1)}, s32[32]{0:T(128)}, u32[]{:S(2)}) copy-start(s32[32]{0:T(128)} %param.28) | copy-start | bytes 388
  18.6 13.3 %copy-start.10 = (s32[32]{0:T(128)S(1)}, s32[32]{0:T(128)}, u32[]{:S(2)}) copy-start(s32[32]{0:T(128)} %param.29) | copy-start | bytes 388
  18.6 193.9 %all-to-all-start = ((bf16[2,32,512,128]{2,3,0,1:T(8,128)(2,1)}), bf16[2,32,512,128]{2,3,0,1:T(8,128)(2,1)}, u32[]{:S(2)}, u32[]{:S(2)}) async-start(bf16[2,32,512,128]{2,3,0,1:T(8,128)(2,1)} %copy.29), calls=%async_computation | async-start | bytes 16777216 | tf_op jit(solution)/shard_map/all_to_all | solution.py:82
  29.5 68.2 %all-gather.3.cloned.1.call-start = ((), (), s32[]{:S(2)}) async-start(), calls=%async_computation.4 | async-start | bytes 1179648 | tf_op jit(solution)/shard_map/all_gather | solution.py:83
  30.2 279.1 %all-gather.5.cloned.1.call-start = ((), (), s32[]{:S(2)}) async-start(), calls=%async_computation.5 | async-start | bytes 2359296 | tf_op jit(solution)/shard_map/all_gather | solution.py:93
  293.3 21.4 %copy-start.2 = (bf16[64,1024]{1,0:T(8,128)(2,1)S(1)}, bf16[64,1024]{1,0:T(8,128)(2,1)}, u32[]{:S(2)}) copy-start(bf16[64,1024]{1,0:T(8,128)(2,1)} %param.16) | copy-start | bytes 393220
  297.4 19.7 %copy-start.3 = (f32[1024]{0:T(1024)S(1)}, f32[1024]{0:T(1024)}, u32[]{:S(2)}) copy-start(f32[1024]{0:T(1024)} %param.24) | copy-start | bytes 12292
  297.4 19.7 %copy-start.4 = (f32[1024]{0:T(1024)S(1)}, f32[1024]{0:T(1024)}, u32[]{:S(2)}) copy-start(f32[1024]{0:T(1024)} %param.23) | copy-start | bytes 12292
  297.4 37.2 %copy-start.8 = (f32[512]{0:T(512)S(1)}, f32[512]{0:T(512)}, u32[]{:S(2)}) copy-start(f32[512]{0:T(512)} %param.20) | copy-start | bytes 6148
  298.5 16.2 %all-to-all-start.1 = ((bf16[8,64,128]{2,1,0:T(8,128)(2,1)}), bf16[8,64,128]{2,1,0:T(8,128)(2,1)S(1)}, u32[]{:S(2)}, u32[]{:S(2)}) async-start(bf16[8,64,128]{2,1,0:T(8,128)(2,1)} %copy.35), calls=%async_computation.1 | async-start | bytes 262144 | tf_op jit(solution)/shard_map/all_to_all | solution.py:109
  334.6 21.1 %copy-start.5 = (f32[1024]{0:T(1024)S(1)}, f32[1024]{0:T(1024)}, u32[]{:S(2)}) copy-start(f32[1024]{0:T(1024)} %param.22) | copy-start | bytes 12292
  339.2 16.9 %copy-start.6 = (f32[1024]{0:T(1024)S(1)}, f32[1024]{0:T(1024)}, u32[]{:S(2)}) copy-start(f32[1024]{0:T(1024)} %param.26) | copy-start | bytes 12292
  339.3 16.9 %copy-start.7 = (f32[1024]{0:T(1024)S(1)}, f32[1024]{0:T(1024)}, u32[]{:S(2)}) copy-start(f32[1024]{0:T(1024)} %param.25) | copy-start | bytes 12292
Sparse Core Ops, SparseCore 0:
  32.1 65.5 all-gather.2
  99.4 98.0 all-gather.4
where the time goes:
time: 365 us; the launch traced here: 364 us
  waiting for transfers between devices  182 us (50%)
  matrix products  48.9 us (13%)
  other arithmetic  34.1 us (9%)
  blocking collectives  33.4 us (9%)
  local copies, waits for them, and re-layouts  29.6 us (8%)
  starting transfers between devices  21.7 us (6%)
  between operations  13.7 us (4%)
    all_to_all x1, waiting for transfers between devices, shards(): lax.all_to_all(kv_cache, 'req', split_axis=1, concat_axis=1, tiled=True)  111 us
    all_gather x1, waiting for transfers between devices, shards(): span_rows = lax.all_gather(tokens, 'tp', axis=0, tiled=True)  64.3 us
    dot_general x9, matrix products, partial_attention(): jnp.einsum('chd,nhd->hcn', queries, key_rows, preferred_element_type=jnp....  24.5 us
    reduce_sum x9, other arithmetic, partial_attention(): weight_sums = jnp.sum(weights.astype(jnp.float32), axis=-1)  21.2 us
    all_to_all x1, blocking collectives, shards(): lax.all_to_all(jnp.broadcast_to(normed[None], (n_tp,) + normed.shape), 't...  17.2 us
    all_to_all x1, blocking collectives, shards(): lax.all_to_all(partial.reshape((n_tp, -1) + partial.shape[1:]), 'tp', spl...  16.2 us
    dot_general x9, matrix products, partial_attention(): jnp.einsum('hcn,nhd->chd', weights, value_rows, preferred_element_type=jn...  15.8 us
    unnamed x24, local copies, waits for them, and re-layouts  12.4 us
  transfers between devices with their start and end apart: 4, of which 3 were waited for; matrix products, arithmetic and copies ran while one was open for 25% of the time, Pallas kernels for 0%

commit v1 on v0

--- a/solution.py
+++ b/solution.py
@@ -106,7 +106,10 @@
         0,
     )
     attention = (blended / jnp.repeat(weight_sums, HEAD_DIM, axis=-1)).astype(jnp.bfloat16)
-    attention = lax.all_to_all(attention, "tp", split_axis=0, concat_axis=1, tiled=True)
+    attention = jnp.concatenate(
+        lax.all_to_all(jnp.stack(jnp.split(attention, lax.axis_size("tp"), axis=0)), "tp", 0, 0),
+        axis=1,
+    )
     projected = jnp.dot(attention, full_out, preferred_element_type=jnp.float32)
     normed = layer_norm(tokens.astype(jnp.float32) + projected, ln1_gain, ln1_bias).astype(
         jnp.bfloat16

time: 365 us -> 370 us (1.014)
  local copies, waits for them, and re-layouts: 29.6 us -> 34.3 us
    unnamed x24 -> x31, local copies, waits for them, and re-layouts: 12.4 us -> 16.6 us
  transfers between devices with their start and end apart: 4 -> 4, of which waited for: 3 -> 3; matrix products, arithmetic and copies ran while one was open for 25% -> 26% of each run, Pallas kernels for 0% -> 0%
where the time goes in v1:
time: 370 us; the launch traced here: 369 us
  waiting for transfers between devices  182 us (49%)
  matrix products  48.9 us (13%)
  local copies, waits for them, and re-layouts  34.3 us (9%)
  other arithmetic  34.1 us (9%)
  blocking collectives  33.4 us (9%)
  starting transfers between devices  21.7 us (6%)
  between operations  13.7 us (4%)
    all_to_all x1, waiting for transfers between devices, shards(): lax.all_to_all(kv_cache, 'req', split_axis=1, concat_axis=1, tiled=True)  111 us
    all_gather x1, waiting for transfers between devices, shards(): span_rows = lax.all_gather(tokens, 'tp', axis=0, tiled=True)  64.3 us
    dot_general x9, matrix products, partial_attention(): jnp.einsum('chd,nhd->hcn', queries, key_rows, preferred_element_type=jnp....  24.5 us
    reduce_sum x9, other arithmetic, partial_attention(): weight_sums = jnp.sum(weights.astype(jnp.float32), axis=-1)  21.2 us
    all_to_all x1, blocking collectives, shards(): lax.all_to_all(jnp.broadcast_to(normed[None], (n_tp,) + normed.shape), 't...  17.2 us
    unnamed x31, local copies, waits for them, and re-layouts  16.6 us
    all_to_all x1, blocking collectives, shards(): lax.all_to_all(partial.reshape((n_tp, -1) + partial.shape[1:]), 'tp', spl...  16.2 us
    dot_general x9, matrix products, partial_attention(): jnp.einsum('hcn,nhd->chd', weights, value_rows, preferred_element_type=jn...  15.8 us
  transfers between devices with their start and end apart: 4, of which 3 were waited for; matrix products, arithmetic and copies ran while one was open for 26% of the time, Pallas kernels for 0%

profile of v1, /device:TPU:8, one launch (start us, length us, event | category | flops | bytes accessed | tf_op | source)
XLA Modules:
  0.0 368.6 jit_solution(18010971147278018790)
XLA Ops:
  6.5 12.1 %copy.36 = bf16[2,32,512,128]{2,3,0,1:T(8,128)(2,1)} copy(bf16[2,32,512,128]{3,2,1,0:T(8,128)(2,1)} %param.27) | data formatting | bytes 16777216 | tf_op args[11]
  18.6 10.9 %all-to-all-start = ((bf16[2,32,512,128]{2,3,0,1:T(8,128)(2,1)}), bf16[2,32,512,128]{2,3,0,1:T(8,128)(2,1)}, u32[]{:S(2)}, u32[]{:S(2)}) async-start(bf16[2,32,512,128]{2,3,0,1:T(8,128)(2,1)} %copy.36), calls=%async_computation | async-start | bytes 16777216 | tf_op jit(solution)/shard_map/all_to_all | solution.py:82
  33.3 64.3 %all-gather.3.cloned.1.call-done = bf16[512,1024]{1,0:T(8,128)(2,1)} async-done(((bf16[64,1024]{1,0:T(8,128)(2,1)}), bf16[512,1024]{1,0:T(8,128)(2,1)}) %all-gather.3.cloned.1.call-update) | async-done | bytes 1048592 | tf_op jit(solution)/shard_map/all_gather | solution.py:83
  101.5 111.0 %all-to-all-done = bf16[2,32,512,128]{2,3,0,1:T(8,128)(2,1)} async-done(((bf16[2,32,512,128]{2,3,0,1:T(8,128)(2,1)}), bf16[2,32,512,128]{2,3,0,1:T(8,128)(2,1)}, u32[]{:S(2)}, u32[]{:S(2)}) %all-to-all-start) | async-done | bytes 8388640 | tf_op jit(solution)/shard_map/all_to_all | solution.py:82
  212.5 5.9 %fusion.93 = (bf16[1,32,512,128]{2,3,0,1:T(8,128)(2,1)}, bf16[1,32,512,128]{2,3,0,1:T(8,128)(2,1)}) fusion(bf16[2,32,512,128]{2,3,0,1:T(8,128)(2,1)} %all-to-all-done), kind=kLoop, calls=%fused_computation.145 | loop fusion | bytes 16777216 | tf_op jit(solution)/shard_map/slice | solution.py:101
  218.4 74.6 %while.14 = (s32[]{:T(128)}, f32[8,4,512,2]{2,1,3,0:T(4,128)S(1)}, f32[8,4,512,2]{2,3,1,0:T(2,128)S(1)}, f32[8,4,512,128]{2,3,1,0:T(8,128)}, s32[8,4]{1,0:T(8,12...) while((s32[]{:T(128)}, f32[8,4,512,2]{2,1,3,0:T(4,128)S(1)}, ...), condition=%wide.region_4.5_spmd, body=%wide.region_1.4_spmd.sunk | while | flops 557838336 | bytes 29612216 | solution.py:56
  219.2 3.0 bitcast_reduce_fusion.2
  222.2 2.6 convert_reduce_fusion.4
  228.6 3.0 bitcast_reduce_fusion.2
  231.6 2.6 convert_reduce_fusion.4
  237.9 3.0 bitcast_reduce_fusion.2
  240.9 2.6 convert_reduce_fusion.4
  243.5 1.9 fusion.114
  247.2 3.0 bitcast_reduce_fusion.2
  250.2 2.6 convert_reduce_fusion.4
  252.8 1.9 fusion.114
  256.5 3.0 bitcast_reduce_fusion.2
  259.5 2.6 convert_reduce_fusion.4
  265.9 3.0 bitcast_reduce_fusion.2
  268.9 2.6 convert_reduce_fusion.4
  275.2 3.0 bitcast_reduce_fusion.2
  278.2 2.6 convert_reduce_fusion.4
  280.8 1.9 fusion.114
  284.5 3.0 bitcast_reduce_fusion.2
  287.5 2.6 convert_reduce_fusion.4
  293.3 4.1 %fusion.12 = f32[512,2,64]{0,2,1:T(8,128)S(1)} fusion(f32[32,512,2,64]{1,3,2,0:T(8,128)} %bitcast.109, f32[1,512,2,64]{1,3,2,0:T(8,128)S(1)} %convolution_bitcast_fusion, f32[33,512,2]{1,2,0:T(2,128)S(1)} %get-tuple-element.114), kind=kLoop, calls=%fused_computation.24 | loop fusion | flops 6422528 | bytes 9048064 | tf_op jit(solution)/shard_map/reduce_sum | solution.py:35
  303.3 10.8 %all-to-all-start.1 = ((bf16[8,64,128]{2,1,0:T(8,128)(2,1)}), bf16[8,64,128]{2,1,0:T(8,128)(2,1)S(1)}, u32[]{:S(2)}, u32[]{:S(2)}) async-start(bf16[8,64,128]{2,1,0:T(8,128)(2,1)} %constant_dynamic-update-slice_fusion.1), calls=%async_computation.1 | async-start | bytes 262144 | tf_op jit(solution)/shard_map/all_to_all | solution.py:110
  314.1 5.4 %all-to-all-done.1 = bf16[8,64,128]{2,1,0:T(8,128)(2,1)S(1)} async-done(((bf16[8,64,128]{2,1,0:T(8,128)(2,1)}), bf16[8,64,128]{2,1,0:T(8,128)(2,1)S(1)}, u32[]{:S(2)}, u32[]{:S(2)}) %all-to-all-start.1) | async-done | bytes 131104 | tf_op jit(solution)/shard_map/all_to_all | solution.py:110
  319.5 2.2 fusion.96
  322.2 17.2 %all_to_all.20 = bf16[8,64,1024]{2,1,0:T(8,128)(2,1)S(1)} all-to-all(bf16[8,64,1024]{2,1,0:T(8,128)(2,1)S(1)} %broadcast_in_dim.109), channel_id=1, replica_groups=mesh['req'=32,'tp'=8] {'tp'}, dimensions={0} | all-to-all | bytes 2097152 | tf_op jit(solution)/shard_map/all_to_all | solution.py:118
  339.4 4.6 %convolution_convert_fusion = bf16[512,1024]{1,0:T(8,128)(2,1)S(1)} fusion(bf16[512,1024]{1,0:T(8,128)(2,1)S(1)} %copy-done, bf16[512,1024]{1,0:T(8,128)(2,1)S(1)} %bitcast.113, bf16[1024,512]{1,0:T(8,128)(2,1)} %param.19, f32[512]{0:T(512)S(1)} %copy-done.8), kind=kOutput, calls=%fused_computation.31 | convolution fusion | flops 1091567616 | bytes 4196352 | tf_op jit(solution)/shard_map/dot_general | solution.py:128
  344.0 16.2 %all_to_all.21 = bf16[8,64,1024]{2,1,0:T(8,128)(2,1)S(1)} all-to-all(bf16[8,64,1024]{2,1,0:T(8,128)(2,1)S(1)} %bitcast.114), channel_id=1, replica_groups=mesh['req'=32,'tp'=8] {'tp'}, dimensions={0} | all-to-all | bytes 2097152 | tf_op jit(solution)/shard_map/all_to_all | solution.py:129
  (119 shorter events, 39.9 us)
Async XLA Ops:
  6.5 332.8 %copy-start = (bf16[512,1024]{1,0:T(8,128)(2,1)S(1)}, bf16[512,1024]{1,0:T(8,128)(2,1)}, u32[]{:S(2)}) copy-start(bf16[512,1024]{1,0:T(8,128)(2,1)} %param.21) | copy-start | bytes 3145732
  18.6 12.4 %copy-start.1 = (bf16[1024,3,128]{2,0,1:T(8,128)(2,1)S(1)}, bf16[1024,3,128]{2,0,1:T(8,128)(2,1)}, u32[]{:S(2)}) copy-start(bf16[1024,3,128]{2,0,1:T(8,128)(2,1)} %param.17) | copy-start | bytes 2359300
  18.6 12.7 %copy-start.9 = (s32[32]{0:T(128)S(1)}, s32[32]{0:T(128)}, u32[]{:S(2)}) copy-start(s32[32]{0:T(128)} %param.28) | copy-start | bytes 388
  18.6 13.3 %copy-start.10 = (s32[32]{0:T(128)S(1)}, s32[32]{0:T(128)}, u32[]{:S(2)}) copy-start(s32[32]{0:T(128)} %param.29) | copy-start | bytes 388
  18.6 193.9 %all-to-all-start = ((bf16[2,32,512,128]{2,3,0,1:T(8,128)(2,1)}), bf16[2,32,512,128]{2,3,0,1:T(8,128)(2,1)}, u32[]{:S(2)}, u32[]{:S(2)}) async-start(bf16[2,32,512,128]{2,3,0,1:T(8,128)(2,1)} %copy.36), calls=%async_computation | async-start | bytes 16777216 | tf_op jit(solution)/shard_map/all_to_all | solution.py:82
  29.5 68.2 %all-gather.3.cloned.1.call-start = ((), (), s32[]{:S(2)}) async-start(), calls=%async_computation.4 | async-start | bytes 1179648 | tf_op jit(solution)/shard_map/all_gather | solution.py:83
  30.2 283.9 %all-gather.5.cloned.1.call-start = ((), (), s32[]{:S(2)}) async-start(), calls=%async_computation.5 | async-start | bytes 2359296 | tf_op jit(solution)/shard_map/all_gather | solution.py:93
  293.3 26.2 %copy-start.2 = (bf16[64,1024]{1,0:T(8,128)(2,1)S(1)}, bf16[64,1024]{1,0:T(8,128)(2,1)}, u32[]{:S(2)}) copy-start(bf16[64,1024]{1,0:T(8,128)(2,1)} %param.16) | copy-start | bytes 393220
  297.4 24.5 %copy-start.3 = (f32[1024]{0:T(1024)S(1)}, f32[1024]{0:T(1024)}, u32[]{:S(2)}) copy-start(f32[1024]{0:T(1024)} %param.24) | copy-start | bytes 12292
  297.4 24.5 %copy-start.4 = (f32[1024]{0:T(1024)S(1)}, f32[1024]{0:T(1024)}, u32[]{:S(2)}) copy-start(f32[1024]{0:T(1024)} %param.23) | copy-start | bytes 12292
  297.4 41.9 %copy-start.8 = (f32[512]{0:T(512)S(1)}, f32[512]{0:T(512)}, u32[]{:S(2)}) copy-start(f32[512]{0:T(512)} %param.20) | copy-start | bytes 6148
  303.3 16.2 %all-to-all-start.1 = ((bf16[8,64,128]{2,1,0:T(8,128)(2,1)}), bf16[8,64,128]{2,1,0:T(8,128)(2,1)S(1)}, u32[]{:S(2)}, u32[]{:S(2)}) async-start(bf16[8,64,128]{2,1,0:T(8,128)(2,1)} %constant_dynamic-update-slice_fusion.1), calls=%async_computation.1 | async-start | bytes 262144 | tf_op jit(solution)/shard_map/all_to_all | solution.py:110
  339.4 21.1 %copy-start.5 = (f32[1024]{0:T(1024)S(1)}, f32[1024]{0:T(1024)}, u32[]{:S(2)}) copy-start(f32[1024]{0:T(1024)} %param.22) | copy-start | bytes 12292
  344.0 16.9 %copy-start.6 = (f32[1024]{0:T(1024)S(1)}, f32[1024]{0:T(1024)}, u32[]{:S(2)}) copy-start(f32[1024]{0:T(1024)} %param.26) | copy-start | bytes 12292
  344.0 16.9 %copy-start.7 = (f32[1024]{0:T(1024)S(1)}, f32[1024]{0:T(1024)}, u32[]{:S(2)}) copy-start(f32[1024]{0:T(1024)} %param.25) | copy-start | bytes 12292
Sparse Core Ops, SparseCore 0:
  32.1 65.5 all-gather.2
  99.4 98.0 all-gather.4
